TPU v7x, 512 devices: a whole 4x8x8 slice. The times are simulated.
512 devices in a mesh: grp: 16 (over z, core), dev: 32 (over x, y).
Axes of the slice: x: 4, y: 8, z: 8, core: 2. Of those that a mesh axis runs over, the one named last changes fastest.
Arguments:
- ssm_input: bfloat16 [4096, 4096], P('grp', 'dev'), may hold values from -6 to 6
- gate_input: bfloat16 [4096, 4096], P('grp', 'dev'), may hold values from -6 to 6
- step_size: float32 [4096, 64], P('grp', 'dev'), may hold values from 6.1035156e-05 to 0.3375
- decay_rate: float32 [64], P('dev'), may hold values from 0.5 to 2
- in_coeff: bfloat16 [4096, 128], P('grp'), may hold values from -6 to 6
- out_coeff: bfloat16 [4096, 128], P('grp'), may hold values from -6 to 6
- skip_gain: float32 [64], P('dev'), may hold values from 0.5 to 3
- norm_gain: float32 [4096], P('dev'), may hold values from 0.5 to 1.5
- out_proj: bfloat16 [4096, 2048], P(None, 'dev'), may hold values from -0.09375 to 0.09375
- residual: bfloat16 [4096, 2048], P(('grp', 'dev')), may hold values from -6 to 6
- ffn_gain: float32 [2048], replicated, may hold values from 0.5 to 1.5
- router: float32 [2048, 16], replicated, may hold values from -0.125 to 0.125
- routes: int32 [4096, 2], P(('grp', 'dev')), may hold values from 0 to 15, all different within a row; in each aligned block of 8 rows (0 to 7, 8 to 15, ...) at most 2 rows name the same one
- gate_weight: bfloat16 [16, 2048, 8192], P('grp', None, 'dev'), may hold values from -0.125 to 0.125
- up_weight: bfloat16 [16, 2048, 8192], P('grp', None, 'dev'), may hold values from -0.125 to 0.125
- down_weight: bfloat16 [16, 8192, 2048], P('grp', 'dev'), may hold values from -0.0625 to 0.0625
Outputs:
- moe_out: bfloat16 [4096, 2048], P(('grp', 'dev'))
Inputs may be any that keep to these rules, and one draw needn't show every extreme that they name: `routes`: each row names two different experts; among the 8 rows of one dispatch block of consecutive tokens no expert is named more than 2 times, a bound that some block reaches.
All inputs are finite; a program needn't handle non-finite values.
Results may differ from a plain program's by a relative error of at most 0.012.
Values may be sent and summed in bfloat16 or wider, within the bound.
No kernel may reach another device: no remote copies, remote signals or barrier semaphores. Data moves between devices by JAX's collectives and lax.ppermute only.
A program may use at most 64 MiB of HBM per device.

v0:
```python
import jax
import jax.numpy as jnp
from jax import lax
from jax.sharding import Mesh
from jax.sharding import PartitionSpec as P

DEV = ("dev_0", "dev_1")
GRP_DEV = ("grp", "dev_0", "dev_1")
EPSILON = 1e-05
HIGHEST_PREC = lax.Precision.HIGHEST


def side_by_side(arrays, axis, dim, along):
    columns = [a.reshape(*a.shape[:along], -1) for a in arrays]
    both = jnp.concatenate(columns, axis=along)
    filled, at, finished = (lax.all_gather(both, axis, axis=dim, tiled=True), 0, [])
    for a, column in zip(arrays, columns):
        piece = filled[..., at : at + column.shape[along]]
        finished.append(piece.reshape(*piece.shape[:along], *a.shape[along:]))
        at += column.shape[along]
    return tuple(finished)


def sent_to_all(shard, axis):
    peers = lax.axis_size(axis)
    return lax.all_to_all(
        jnp.broadcast_to(shard[None], (peers, *shard.shape)), axis, 0, 0, tiled=True
    )


def of_everyone(shard, axis):
    everything = sent_to_all(shard, axis)
    return jnp.sum(everything, axis=0)


def in_order(tiles, dim):
    dims = list(tiles.shape[1:])
    dims[dim] *= tiles.shape[0]
    return jnp.moveaxis(tiles, 0, dim).reshape(dims)


def collect(shard, axis, dim):
    return in_order(sent_to_all(shard, axis), dim)


def sum_by_axis(terms, axes):
    total = terms.astype(jnp.bfloat16)
    total = lax.psum_scatter(total, axes, scatter_dimension=0, tiled=True)
    return total.astype(jnp.float32)


def rms_scale(values, gain_vec):
    return (
        values * lax.rsqrt(jnp.mean(values * values, axis=-1, keepdims=True) + EPSILON) * gain_vec
    )


def slot_tables(routes_block, expert_count, slot_cap):
    blocks, row_total = (routes_block.shape[0], routes_block.shape[1])
    flat_routes = routes_block.reshape(blocks, row_total * 2)
    onehot = (
        flat_routes[:, :, None] == jnp.arange(expert_count, dtype=jnp.int32)[None, None, :]
    ).astype(jnp.int32)
    earlier = jnp.cumsum(onehot, axis=1) - onehot
    slot_rank = jnp.sum(earlier * onehot, axis=2)
    slot_index = (flat_routes * slot_cap + slot_rank).reshape(blocks, row_total, 2)
    placed = (
        slot_index[:, :, :, None]
        == jnp.arange(expert_count * slot_cap, dtype=jnp.int32)[None, None, None, :]
    )
    return placed.astype(jnp.float32)


def shards(
    ssm_input,
    gate_input,
    step_size,
    decay_rate,
    in_coeff,
    out_coeff,
    skip_gain,
    norm_gain,
    out_proj,
    residual,
    ffn_gain,
    router,
    routes,
    gate_weight,
    up_weight,
    down_weight,
):
    tok_rows = ssm_input.shape[0]
    head_count = step_size.shape[1]
    head_width = ssm_input.shape[1] // head_count
    dev_count = lax.axis_size(DEV)
    inner_dim = ssm_input.shape[1] * dev_count
    block_rows = residual.shape[0]
    model_dim = residual.shape[1]
    experts = lax.axis_size("grp")
    slot_cap = max(2, 4 * block_rows // experts)
    group_slots = experts * slot_cap
    inputs_f = ssm_input.astype(jnp.float32).reshape(tok_rows, head_count, head_width)
    in_float = in_coeff.astype(jnp.float32)
    out_float = out_coeff.astype(jnp.float32)
    log_rate = -(step_size * decay_rate[None, :])
    cumulative = jnp.cumsum(log_rate, axis=0)
    causal = (jnp.arange(tok_rows)[:, None] >= jnp.arange(tok_rows)[None, :])[:, :, None]
    spread = cumulative[:, None, :] - cumulative[None, :, :]
    decay_pair = jnp.where(causal, jnp.exp(jnp.where(causal, spread, 0.0)), 0.0)
    scores = jnp.dot(out_coeff, in_coeff.T, preferred_element_type=jnp.float32)
    mixing = decay_pair * scores[:, :, None] * step_size[None, :, :]
    inside = jnp.einsum("tuh,uhp->thp", mixing, inputs_f, precision=HIGHEST_PREC)
    to_end = jnp.exp(cumulative[-1][None, :] - cumulative) * step_size
    own_state = jnp.einsum("uh,uhp,un->hpn", to_end, inputs_f, in_float, precision=HIGHEST_PREC)
    own_log = cumulative[-1]
    group_logs, group_states = tuple(
        (
            part.astype(jnp.float32)
            for part in side_by_side(
                (own_log[None].astype(jnp.bfloat16), own_state[None].astype(jnp.bfloat16)),
                "grp",
                0,
                2,
            )
        )
    )
    group_index = jnp.arange(group_logs.shape[0])
    my_group = lax.axis_index("grp")
    inclusive = jnp.cumsum(group_logs, axis=0)
    exclusive = inclusive - group_logs
    before_me = jnp.sum(jnp.where((group_index == my_group)[:, None], exclusive, 0.0), axis=0)
    earlier_mask = (group_index < my_group)[:, None]
    weighting = jnp.where(
        earlier_mask, jnp.exp(jnp.where(earlier_mask, before_me[None, :] - inclusive, 0.0)), 0.0
    )
    entering = jnp.einsum("gh,ghpn->hpn", weighting, group_states, precision=HIGHEST_PREC)
    carried = jnp.exp(cumulative)[:, :, None] * jnp.einsum(
        "hpn,tn->thp", entering, out_float, precision=HIGHEST_PREC
    )
    ssm_out = inside + carried + skip_gain[None, :, None] * inputs_f
    gated_out = ssm_out.reshape(tok_rows, head_count * head_width) * jax.nn.silu(
        gate_input.astype(jnp.float32)
    )
    squares = lax.psum(jnp.sum(gated_out * gated_out, axis=1), DEV)
    mixed_rows = (
        gated_out * lax.rsqrt(squares[:, None] / inner_dim + EPSILON) * norm_gain[None, :]
    ).astype(jnp.bfloat16)
    gathered = lax.all_gather(mixed_rows, DEV, axis=0)
    projected = jnp.einsum(
        "dtc,dcf->tf",
        gathered,
        out_proj.reshape(dev_count, -1, out_proj.shape[1]),
        preferred_element_type=jnp.float32,
    ).astype(jnp.bfloat16)
    mamba_out = lax.all_to_all(projected, DEV, split_axis=0, concat_axis=1, tiled=True)
    hidden_res = (residual.astype(jnp.float32) + mamba_out.astype(jnp.float32)).astype(jnp.bfloat16)
    hidden_float = hidden_res.astype(jnp.float32)
    normed = rms_scale(hidden_float, ffn_gain).astype(jnp.bfloat16)
    logits = jnp.dot(normed.astype(jnp.float32), router, precision=HIGHEST_PREC)
    expert_ids = jnp.arange(experts, dtype=jnp.int32)[None, :]
    first_logit = jnp.sum(logits * (routes[:, 0:1] == expert_ids).astype(jnp.float32), axis=1)
    second_logit = jnp.sum(logits * (routes[:, 1:2] == expert_ids).astype(jnp.float32), axis=1)
    first_prob = jax.nn.sigmoid(first_logit - second_logit)
    second_prob = 1.0 - first_prob
    placed = slot_tables(routes[None], experts, slot_cap)[0]
    filled = jnp.sum(placed, axis=1)
    outgoing = jnp.dot(
        filled.T.astype(jnp.bfloat16), normed, preferred_element_type=jnp.float32
    ).astype(jnp.bfloat16)
    outgoing = outgoing.reshape(experts, slot_cap, model_dim)
    arrived = lax.all_to_all(outgoing, "grp", split_axis=0, concat_axis=0, tiled=True)
    all_rows = lax.all_gather(arrived, DEV, axis=0, tiled=True).reshape(-1, model_dim)
    gate_act = jnp.dot(all_rows, gate_weight[0], preferred_element_type=jnp.float32)
    up_act = jnp.dot(all_rows, up_weight[0], preferred_element_type=jnp.float32)
    hidden = (jax.nn.silu(gate_act) * up_act).astype(jnp.bfloat16)
    summed = sum_by_axis(jnp.dot(hidden, down_weight[0], preferred_element_type=jnp.float32), DEV)
    returned = lax.all_to_all(
        summed.astype(jnp.bfloat16).reshape(experts, slot_cap, model_dim),
        "grp",
        split_axis=0,
        concat_axis=0,
        tiled=True,
    )
    weights = first_prob[:, None] * placed[:, 0, :] + second_prob[:, None] * placed[:, 1, :]
    contrib = jnp.dot(
        weights,
        returned.reshape(group_slots, model_dim).astype(jnp.float32),
        precision=HIGHEST_PREC,
    )
    return (hidden_float + contrib).astype(jnp.bfloat16)


def solution(mesh):
    torus = Mesh(mesh.devices.reshape(mesh.shape["grp"], 4, 8), ("grp", "dev_0", "dev_1"))
    in_specs = (
        P("grp", DEV),
        P("grp", DEV),
        P("grp", DEV),
        P(DEV),
        P("grp", None),
        P("grp", None),
        P(DEV),
        P(DEV),
        P(None, DEV),
        P(GRP_DEV, None),
        P(),
        P(),
        P(GRP_DEV, None),
        P("grp", None, DEV),
        P("grp", None, DEV),
        P("grp", DEV, None),
    )
    out_specs = P(GRP_DEV, None)
    return jax.shard_map(
        shards, mesh=torus, in_specs=in_specs, out_specs=out_specs, check_vma=False
    )
```

profile of v0, /device:TPU:1, one launch (start us, length us, event | category | flops | bytes accessed | tf_op | source)
XLA Modules:
  0.0 574.6 jit_solution(1486846018110611630)
XLA Ops:
  6.6 0.9 negate_bitcast_fusion
  7.5 0.6 reduce-window.6
  8.1 0.2 slice_reduce_fusion
  8.3 0.2 reduce-window.9
  8.5 0.2 slice_reduce_fusion.1
  8.8 0.8 fusion.58
  9.5 0.9 copy.61
  10.5 1.0 convolution_convert_fusion.2
  11.6 0.1 pad_maximum_fusion
  11.7 26.0 %all_gather.12 = bf16[16,2,8193]{2,1,0:T(2,128)(2,1)S(1)} all-gather(bf16[1,2,8193]{2,1,0:T(2,128)(2,1)S(1)} %pad_maximum_fusion), channel_id=1, replica_groups=mesh['grp'=16,'dev_0'=4,'dev_1'=8] {'grp'}, dimensions={0}, use_global_device_ids=true | all-gather | bytes 557124 | tf_op jit(solution)/shard_map/all_gather | solution.py:16
  37.6 0.7 slice.40
  38.4 0.1 copy.76
  38.5 0.1 copy.64
  38.6 0.1 select_reduce_fusion.1
  38.8 0.1 copy.73
  38.9 0.4 reshape.234
  39.3 1.1 fusion.59
  40.3 0.6 fusion.18
  40.9 0.2 fusion.4
  41.2 0.6 fusion.3
  41.8 0.1 copy.66
  41.9 0.1 multiply_reduce_fusion
  42.0 61.3 %psum.7 = f32[256]{0:T(256)S(1)} all-reduce(f32[256]{0:T(256)S(1)} %multiply_reduce_fusion), channel_id=1, replica_groups=mesh['grp'=16,'dev_0'=4,'dev_1'=8] {'dev_0','dev_1'}, use_global_device_ids=true, to_apply=%region_5.6 | all-reduce | flops 256 | bytes 2048 | tf_op jit(solution)/shard_map/psum | solution.py:144
  103.4 0.7 multiply_convert_fusion
  104.4 0.2 select_reduce_fusion
  104.7 0.1 copy.72
  104.7 81.8 %all-gather.6.cloned.1.call-done = bf16[8192,128]{1,0:T(8,128)(2,1)} async-done(((bf16[256,128]{1,0:T(8,128)(2,1)}), bf16[8192,128]{1,0:T(8,128)(2,1)}) %all-gather.6.cloned.1.call-update) | async-done | bytes 2097168 | tf_op jit(solution)/shard_map/all_gather | solution.py:148
  186.6 2.3 fusion.5
  188.9 0.1 copy.68
  189.1 0.7 reshape.251
  189.8 4.9 all-to-all-start
  194.9 8.6 %all-to-all-done = bf16[32,2,256]{2,1,0:T(2,128)(2,1)S(1)} async-done(((bf16[32,2,256]{2,1,0:T(2,128)(2,1)}), bf16[32,2,256]{2,1,0:T(2,128)(2,1)S(1)}, u32[]{:S(2)}, u32[]{:S(2)}) %all-to-all-start) | async-done | bytes 32800 | tf_op jit(solution)/shard_map/all_to_all | solution.py:155
  203.5 0.1 reshape.252
  203.7 0.1 reshape.242
  203.8 0.1 fusion.37
  203.9 0.2 convolution_convert_fusion.1
  204.2 0.1 reshape.237
  204.3 22.8 %all_to_all.23 = bf16[16,2,2048]{2,1,0:T(2,128)(2,1)} all-to-all(bf16[16,2,2048]{2,1,0:T(2,128)(2,1)S(1)} %reshape.237), channel_id=1, replica_groups=mesh['grp'=16,'dev_0'=4,'dev_1'=8] {'grp'}, dimensions={0} | all-to-all | bytes 262144 | tf_op jit(solution)/shard_map/all_to_all | solution.py:171
  227.1 73.9 %all-gather.4.cloned.1.call-done = bf16[512,2,2048]{2,1,0:T(2,128)(2,1)} async-done(((bf16[16,2,2048]{2,1,0:T(2,128)(2,1)}), bf16[512,2,2048]{2,1,0:T(2,128)(2,1)}) %all-gather.4.cloned.1.call-update) | async-done | bytes 4194320 | tf_op jit(solution)/shard_map/all_gather | solution.py:172
  301.0 7.2 %reshape.238 = bf16[1024,2048]{1,0:T(8,128)(2,1)} reshape(bf16[512,2,2048]{2,1,0:T(2,128)(2,1)} %all-gather.4.cloned.1.call-done) | data formatting | bytes 8388608 | tf_op jit(solution)/shard_map/reshape | solution.py:172
  308.2 4.5 fusion.9
  312.8 9.1 %convolution_convert_fusion = bf16[1024,2048]{1,0:T(8,128)(2,1)} fusion(bf16[1024,2048]{1,0:T(8,128)(2,1)} %reshape.238, bf16[1,256,2048]{2,1,0:T(8,128)(2,1)S(1)} %copy-done, bf16[1,2048,256]{2,1,0:T(8,128)(2,1)} %param.30, f32[1024,256]{1,0:T(8,128)} %fusion.9), kind=kOutput, calls=%fused_computation | convolution fusion | flops 2151153664 | bytes 11534336 | tf_op jit(solution)/shard_map/dot_general | solution.py:176
  322.0 222.0 %reduce-scatter.2.cloned.1.call-done = bf16[32,2048]{1,0:T(8,128)(2,1)} async-done(((bf16[1024,2048]{1,0:T(8,128)(2,1)}), bf16[32,2048]{1,0:T(8,128)(2,1)}) %reduce-scatter.2.cloned.1.call-update) | async-done | bytes 131088 | tf_op jit(solution)/shard_map/reduce_scatter | solution.py:48
  544.0 1.7 reshape.239
  545.6 12.4 %all-to-all-start.2 = ((bf16[16,2,2048]{2,1,0:T(2,128)(2,1)}), bf16[16,2,2048]{2,1,0:T(2,128)(2,1)S(1)}, u32[]{:S(2)}, u32[]{:S(2)}) async-start(bf16[16,2,2048]{2,1,0:T(2,128)(2,1)} %reshape.239), calls=%async_computation.3 | async-start | bytes 262144 | tf_op jit(solution)/shard_map/all_to_all | solution.py:177
  558.0 0.3 select_reduce_fusion.2
  558.4 8.8 %all-to-all-done.2 = bf16[16,2,2048]{2,1,0:T(2,128)(2,1)S(1)} async-done(((bf16[16,2,2048]{2,1,0:T(2,128)(2,1)}), bf16[16,2,2048]{2,1,0:T(2,128)(2,1)S(1)}, u32[]{:S(2)}, u32[]{:S(2)}) %all-to-all-start.2) | async-done | bytes 131104 | tf_op jit(solution)/shard_map/all_to_all | solution.py:177
  567.2 0.9 fusion
  (56 shorter events, 1.2 us)
Async XLA Ops:
  6.5 306.2 %copy-start = (bf16[1,256,2048]{2,1,0:T(8,128)(2,1)S(1)}, bf16[1,256,2048]{2,1,0:T(8,128)(2,1)}, u32[]{:S(2)}) copy-start(bf16[1,256,2048]{2,1,0:T(8,128)(2,1)} %param.31) | copy-start | bytes 3145732
  6.5 34.6 %copy-start.6 = (f32[256,2]{0,1:T(2,128)S(1)}, f32[256,2]{0,1:T(2,128)}, u32[]{:S(2)}) copy-start(f32[256,2]{0,1:T(2,128)} %param.18) | copy-start | bytes 6148
  6.5 34.4 %copy-start.3 = (bf16[256,128]{1,0:T(8,128)(2,1)S(1)}, bf16[256,128]{1,0:T(8,128)(2,1)}, u32[]{:S(2)}) copy-start(bf16[256,128]{1,0:T(8,128)(2,1)} %param.21) | copy-start | bytes 196612
  6.5 34.6 %copy-start.11 = (f32[2]{0:T(128)S(1)}, f32[2]{0:T(128)}, u32[]{:S(2)}) copy-start(f32[2]{0:T(128)} %param.22) | copy-start | bytes 28
  6.5 35.3 %copy-start.2 = (bf16[256,128]{1,0:T(8,128)(2,1)S(1)}, bf16[256,128]{1,0:T(8,128)(2,1)}, u32[]{:S(2)}) copy-start(bf16[256,128]{1,0:T(8,128)(2,1)} %param.17) | copy-start | bytes 196612
  6.5 96.8 %copy-start.8 = (f32[128]{0:T(128)S(1)}, f32[128]{0:T(128)}, u32[]{:S(2)}) copy-start(f32[128]{0:T(128)} %param.23) | copy-start | bytes 1540
  6.6 97.5 %copy-start.7 = (s32[8,2]{0,1:T(2,128)S(1)}, s32[8,2]{0,1:T(2,128)}, u32[]{:S(2)}) copy-start(s32[8,2]{0,1:T(2,128)} %param.28) | copy-start | bytes 196
  6.6 180.0 %copy-start.1 = (bf16[4096,64]{0,1:T(8,128)(2,1)S(1)}, bf16[4096,64]{0,1:T(8,128)(2,1)}, u32[]{:S(2)}) copy-start(bf16[4096,64]{0,1:T(8,128)(2,1)} %param.24) | copy-start | bytes 1572868
  6.6 180.0 %all-gather.6.cloned.1.call-start = ((), (), s32[]{:S(2)}) async-start(), calls=%async_computation.6 | async-start | bytes 2162688 | tf_op jit(solution)/shard_map/all_gather | solution.py:148
  38.3 165.4 %copy-start.4 = (bf16[8,2048]{1,0:T(8,128)(2,1)S(1)}, bf16[8,2048]{1,0:T(8,128)(2,1)}, u32[]{:S(2)}) copy-start(bf16[8,2048]{1,0:T(8,128)(2,1)} %param.25) | copy-start | bytes 98308
  38.7 165.2 %copy-start.5 = (f32[2048]{0:T(1024)S(1)}, f32[2048]{0:T(1024)}, u32[]{:S(2)}) copy-start(f32[2048]{0:T(1024)} %param.26) | copy-start | bytes 24580
  189.8 13.7 %all-to-all-start = ((bf16[32,2,256]{2,1,0:T(2,128)(2,1)}), bf16[32,2,256]{2,1,0:T(2,128)(2,1)S(1)}, u32[]{:S(2)}, u32[]{:S(2)}) async-start(bf16[32,2,256]{2,1,0:T(2,128)(2,1)} %reshape.251), calls=%async_computation | async-start | bytes 65536 | tf_op jit(solution)/shard_map/all_to_all | solution.py:155
  194.7 106.3 %all-gather.4.cloned.1.call-start = ((), (), s32[]{:S(2)}) async-start(), calls=%async_computation.4 | async-start | bytes 4325376 | tf_op jit(solution)/shard_map/all_gather | solution.py:172
  227.1 81.2 %copy-start.9 = (bf16[1,2048,256]{2,1,0:T(8,128)(2,1)S(1)}, bf16[1,2048,256]{2,1,0:T(8,128)(2,1)}, u32[]{:S(2)}) copy-start(bf16[1,2048,256]{2,1,0:T(8,128)(2,1)} %param.29) | copy-start | bytes 3145732
  227.1 316.9 %reduce-scatter.2.cloned.1.call-start = ((), (), s32[]{:S(2)}) async-start(), calls=%async_computation.5 | async-start | bytes 4325376 | tf_op jit(solution)/shard_map/reduce_scatter | solution.py:48
  321.9 236.1 %copy-start.10 = (f32[2048,16]{0,1:T(8,128)S(1)}, f32[2048,16]{0,1:T(8,128)}, u32[]{:S(2)}) copy-start(f32[2048,16]{0,1:T(8,128)} %param.27) | copy-start | bytes 393220
  545.6 21.6 %all-to-all-start.2 = ((bf16[16,2,2048]{2,1,0:T(2,128)(2,1)}), bf16[16,2,2048]{2,1,0:T(2,128)(2,1)S(1)}, u32[]{:S(2)}, u32[]{:S(2)}) async-start(bf16[16,2,2048]{2,1,0:T(2,128)(2,1)} %reshape.239), calls=%async_computation.3 | async-start | bytes 262144 | tf_op jit(solution)/shard_map/all_to_all | solution.py:177
Sparse Core Ops, SparseCore 0:
  104.2 82.3 all-gather.5
  227.2 73.7 all-gather.3
  322.0 221.9 reduce-scatter.1
where the time goes:
time: 575 us
  waiting for transfers between devices  395 us (69%)
  blocking collectives  110 us (19%)
  matrix products  20.9 us (4%)
  starting transfers between devices  17.4 us (3%)
  between operations  13.4 us (2%)
  local copies, waits for them, and re-layouts  13.3 us (2%)
    reduce_scatter x1, waiting for transfers between devices, sum_by_axis(): total = lax.psum_scatter(total, axes, scatter_dimension=0, tiled=True)  222 us
    all_gather x1, waiting for transfers between devices, shards(): gathered = lax.all_gather(mixed_rows, DEV, axis=0)  81.8 us
    all_gather x1, waiting for transfers between devices, shards(): lax.all_gather(arrived, DEV, axis=0, tiled=True).reshape(-1, model_dim)  73.9 us
    psum x1, blocking collectives, shards(): squares = lax.psum(jnp.sum(gated_out * gated_out, axis=1), DEV)  61.3 us
    all_gather x1, blocking collectives, side_by_side(): lax.all_gather(both, axis, axis=dim, tiled=True)  26 us
    all_to_all x1, blocking collectives, shards(): lax.all_to_all(outgoing, 'grp', split_axis=0, concat_axis=0, tiled=True)  22.8 us
    all_to_all x1, starting transfers between devices, shards(): lax.all_to_all(summed.astype(jnp.bfloat16).reshape(experts, slot_cap, mod...  12.4 us
  transfers between devices with their start and end apart: 5, of which 5 were waited for; matrix products, arithmetic and copies ran while one was open for 0% of the time, Pallas kernels for 0%

commit v1 on v0

--- a/solution.py
+++ b/solution.py
@@ -141,7 +141,7 @@
     gated_out = ssm_out.reshape(tok_rows, head_count * head_width) * jax.nn.silu(
         gate_input.astype(jnp.float32)
     )
-    squares = lax.psum(jnp.sum(gated_out * gated_out, axis=1), DEV)
+    squares = jnp.sum(lax.all_gather(jnp.sum(gated_out * gated_out, axis=1), DEV), axis=0)
     mixed_rows = (
         gated_out * lax.rsqrt(squares[:, None] / inner_dim + EPSILON) * norm_gain[None, :]
     ).astype(jnp.bfloat16)

time: 575 us -> 544 us (0.946)
  blocking collectives: 110 us -> 79.6 us
    psum x1 -> x0, blocking collectives: 61.3 us -> none  [shards(): squares = lax.psum(jnp.sum(gated_out * gated_out, axis=1), DEV)]
    all_gather x0 -> x1, blocking collectives: none -> 30.9 us  [shards(): lax.all_gather(jnp.sum(gated_out * gated_out, axis=1), DEV)]
where the time goes in v1:
time: 544 us; the launch traced here: 543 us
  waiting for transfers between devices  394 us (72%)
  blocking collectives  79.6 us (15%)
  matrix products  20.9 us (4%)
  starting transfers between devices  17.9 us (3%)
  between operations  13.4 us (2%)
  local copies, waits for them, and re-layouts  13.3 us (2%)
    reduce_scatter x1, waiting for transfers between devices, sum_by_axis(): total = lax.psum_scatter(total, axes, scatter_dimension=0, tiled=True)  221 us
    all_gather x1, waiting for transfers between devices, shards(): gathered = lax.all_gather(mixed_rows, DEV, axis=0)  80.8 us
    all_gather x1, waiting for transfers between devices, shards(): lax.all_gather(arrived, DEV, axis=0, tiled=True).reshape(-1, model_dim)  73.9 us
    all_gather x1, blocking collectives, shards(): lax.all_gather(jnp.sum(gated_out * gated_out, axis=1), DEV)  30.9 us
    all_gather x1, blocking collectives, side_by_side(): lax.all_gather(both, axis, axis=dim, tiled=True)  26 us
    all_to_all x1, blocking collectives, shards(): lax.all_to_all(outgoing, 'grp', split_axis=0, concat_axis=0, tiled=True)  22.8 us
    all_to_all x1, starting transfers between devices, shards(): lax.all_to_all(summed.astype(jnp.bfloat16).reshape(experts, slot_cap, mod...  12.8 us
  transfers between devices with their start and end apart: 5, of which 5 were waited for; matrix products, arithmetic and copies ran while one was open for 0% of the time, Pallas kernels for 0%

profile of v1, /device:TPU:1, one launch (start us, length us, event | category | flops | bytes accessed | tf_op | source)
XLA Modules:
  0.0 543.1 jit_solution(7835378679500422201)
XLA Ops:
  6.6 0.9 negate_bitcast_fusion
  7.5 0.6 reduce-window.6
  8.1 0.2 slice_reduce_fusion
  8.3 0.2 reduce-window.9
  8.5 0.2 slice_reduce_fusion.1
  8.8 0.8 fusion.58
  9.5 0.9 copy.61
  10.5 1.0 convolution_convert_fusion.2
  11.6 0.1 pad_maximum_fusion
  11.7 26.0 %all_gather.18 = bf16[16,2,8193]{2,1,0:T(2,128)(2,1)S(1)} all-gather(bf16[1,2,8193]{2,1,0:T(2,128)(2,1)S(1)} %pad_maximum_fusion), channel_id=1, replica_groups=mesh['grp'=16,'dev_0'=4,'dev_1'=8] {'grp'}, dimensions={0}, use_global_device_ids=true | all-gather | bytes 557124 | tf_op jit(solution)/shard_map/all_gather | solution.py:16
  37.6 0.7 slice.40
  38.4 0.1 copy.76
  38.5 0.1 copy.64
  38.6 0.1 select_reduce_fusion.1
  38.8 0.1 copy.73
  38.9 0.4 reshape.238
  39.3 1.1 fusion.59
  40.3 0.6 fusion.18
  40.9 0.2 fusion.4
  41.2 0.6 fusion.3
  41.8 0.1 copy.66
  41.9 0.1 multiply_reduce_fusion
  42.0 30.9 %all-gather.2 = f32[32,1,256]{2,1,0:T(1,128)S(1)} all-gather(f32[1,1,256]{2,1,0:T(1,128)S(1)} %bitcast.96), channel_id=2, replica_groups=mesh['grp'=16,'dev_0'=4,'dev_1'=8] {'dev_0','dev_1'}, dimensions={0}, use_global_device_ids=true | all-gather | bytes 33792 | tf_op jit(solution)/shard_map/all_gather | solution.py:144
  73.0 0.7 multiply_convert_fusion
  74.1 0.2 select_reduce_fusion
  74.3 0.1 copy.72
  74.4 80.8 %all-gather.8.cloned.1.call-done = bf16[8192,128]{1,0:T(8,128)(2,1)} async-done(((bf16[256,128]{1,0:T(8,128)(2,1)}), bf16[8192,128]{1,0:T(8,128)(2,1)}) %all-gather.8.cloned.1.call-update) | async-done | bytes 2097168 | tf_op jit(solution)/shard_map/all_gather | solution.py:148
  155.2 2.3 fusion.5
  157.5 0.1 copy.68
  157.6 0.7 reshape.259
  158.4 4.9 all-to-all-start
  163.5 8.6 %all-to-all-done = bf16[32,2,256]{2,1,0:T(2,128)(2,1)S(1)} async-done(((bf16[32,2,256]{2,1,0:T(2,128)(2,1)}), bf16[32,2,256]{2,1,0:T(2,128)(2,1)S(1)}, u32[]{:S(2)}, u32[]{:S(2)}) %all-to-all-start) | async-done | bytes 32800 | tf_op jit(solution)/shard_map/all_to_all | solution.py:155
  172.1 0.1 reshape.260
  172.3 0.1 reshape.246
  172.4 0.1 fusion.37
  172.5 0.2 convolution_convert_fusion.1
  172.8 0.1 reshape.241
  172.9 22.8 %all_to_all.23 = bf16[16,2,2048]{2,1,0:T(2,128)(2,1)} all-to-all(bf16[16,2,2048]{2,1,0:T(2,128)(2,1)S(1)} %reshape.241), channel_id=1, replica_groups=mesh['grp'=16,'dev_0'=4,'dev_1'=8] {'grp'}, dimensions={0} | all-to-all | bytes 262144 | tf_op jit(solution)/shard_map/all_to_all | solution.py:171
  195.7 73.9 %all-gather.6.cloned.1.call-done = bf16[512,2,2048]{2,1,0:T(2,128)(2,1)} async-done(((bf16[16,2,2048]{2,1,0:T(2,128)(2,1)}), bf16[512,2,2048]{2,1,0:T(2,128)(2,1)}) %all-gather.6.cloned.1.call-update) | async-done | bytes 4194320 | tf_op jit(solution)/shard_map/all_gather | solution.py:172
  269.6 7.2 %reshape.242 = bf16[1024,2048]{1,0:T(8,128)(2,1)} reshape(bf16[512,2,2048]{2,1,0:T(2,128)(2,1)} %all-gather.6.cloned.1.call-done) | data formatting | bytes 8388608 | tf_op jit(solution)/shard_map/reshape | solution.py:172
  276.8 4.5 fusion.9
  281.3 9.1 %convolution_convert_fusion = bf16[1024,2048]{1,0:T(8,128)(2,1)} fusion(bf16[1024,2048]{1,0:T(8,128)(2,1)} %reshape.242, bf16[1,256,2048]{2,1,0:T(8,128)(2,1)S(1)} %copy-done, bf16[1,2048,256]{2,1,0:T(8,128)(2,1)} %param.30, f32[1024,256]{1,0:T(8,128)} %fusion.9), kind=kOutput, calls=%fused_computation | convolution fusion | flops 2151153664 | bytes 11534336 | tf_op jit(solution)/shard_map/dot_general | solution.py:176
  290.6 221.4 %reduce-scatter.2.cloned.1.call-done = bf16[32,2048]{1,0:T(8,128)(2,1)} async-done(((bf16[1024,2048]{1,0:T(8,128)(2,1)}), bf16[32,2048]{1,0:T(8,128)(2,1)}) %reduce-scatter.2.cloned.1.call-update) | async-done | bytes 131088 | tf_op jit(solution)/shard_map/reduce_scatter | solution.py:48
  512.0 1.7 reshape.243
  513.6 12.8 %all-to-all-start.2 = ((bf16[16,2,2048]{2,1,0:T(2,128)(2,1)}), bf16[16,2,2048]{2,1,0:T(2,128)(2,1)S(1)}, u32[]{:S(2)}, u32[]{:S(2)}) async-start(bf16[16,2,2048]{2,1,0:T(2,128)(2,1)} %reshape.243), calls=%async_computation.3 | async-start | bytes 262144 | tf_op jit(solution)/shard_map/all_to_all | solution.py:177
  526.5 0.3 select_reduce_fusion.2
  526.8 8.8 %all-to-all-done.2 = bf16[16,2,2048]{2,1,0:T(2,128)(2,1)S(1)} async-done(((bf16[16,2,2048]{2,1,0:T(2,128)(2,1)}), bf16[16,2,2048]{2,1,0:T(2,128)(2,1)S(1)}, u32[]{:S(2)}, u32[]{:S(2)}) %all-to-all-start.2) | async-done | bytes 131104 | tf_op jit(solution)/shard_map/all_to_all | solution.py:177
  535.7 0.9 fusion
  (57 shorter events, 1.3 us)
Async XLA Ops:
  6.5 274.8 %copy-start = (bf16[1,256,2048]{2,1,0:T(8,128)(2,1)S(1)}, bf16[1,256,2048]{2,1,0:T(8,128)(2,1)}, u32[]{:S(2)}) copy-start(bf16[1,256,2048]{2,1,0:T(8,128)(2,1)} %param.31) | copy-start | bytes 3145732
  6.5 34.6 %copy-start.6 = (f32[256,2]{0,1:T(2,128)S(1)}, f32[256,2]{0,1:T(2,128)}, u32[]{:S(2)}) copy-start(f32[256,2]{0,1:T(2,128)} %param.18) | copy-start | bytes 6148
  6.5 34.4 %copy-start.3 = (bf16[256,128]{1,0:T(8,128)(2,1)S(1)}, bf16[256,128]{1,0:T(8,128)(2,1)}, u32[]{:S(2)}) copy-start(bf16[256,128]{1,0:T(8,128)(2,1)} %param.21) | copy-start | bytes 196612
  6.5 34.6 %copy-start.11 = (f32[2]{0:T(128)S(1)}, f32[2]{0:T(128)}, u32[]{:S(2)}) copy-start(f32[2]{0:T(128)} %param.22) | copy-start | bytes 28
  6.5 35.3 %copy-start.2 = (bf16[256,128]{1,0:T(8,128)(2,1)S(1)}, bf16[256,128]{1,0:T(8,128)(2,1)}, u32[]{:S(2)}) copy-start(bf16[256,128]{1,0:T(8,128)(2,1)} %param.17) | copy-start | bytes 196612
  6.5 66.5 %copy-start.8 = (f32[128]{0:T(128)S(1)}, f32[128]{0:T(128)}, u32[]{:S(2)}) copy-start(f32[128]{0:T(128)} %param.23) | copy-start | bytes 1540
  6.6 67.2 %copy-start.7 = (s32[8,2]{0,1:T(2,128)S(1)}, s32[8,2]{0,1:T(2,128)}, u32[]{:S(2)}) copy-start(s32[8,2]{0,1:T(2,128)} %param.28) | copy-start | bytes 196
  6.6 148.6 %copy-start.1 = (bf16[4096,64]{0,1:T(8,128)(2,1)S(1)}, bf16[4096,64]{0,1:T(8,128)(2,1)}, u32[]{:S(2)}) copy-start(bf16[4096,64]{0,1:T(8,128)(2,1)} %param.24) | copy-start | bytes 1572868
  6.6 148.6 %all-gather.8.cloned.1.call-start = ((), (), s32[]{:S(2)}) async-start(), calls=%async_computation.6 | async-start | bytes 2162688 | tf_op jit(solution)/shard_map/all_gather | solution.py:148
  38.4 134.0 %copy-start.4 = (bf16[8,2048]{1,0:T(8,128)(2,1)S(1)}, bf16[8,2048]{1,0:T(8,128)(2,1)}, u32[]{:S(2)}) copy-start(bf16[8,2048]{1,0:T(8,128)(2,1)} %param.25) | copy-start | bytes 98308
  38.9 133.6 %copy-start.5 = (f32[2048]{0:T(1024)S(1)}, f32[2048]{0:T(1024)}, u32[]{:S(2)}) copy-start(f32[2048]{0:T(1024)} %param.26) | copy-start | bytes 24580
  158.4 13.7 %all-to-all-start = ((bf16[32,2,256]{2,1,0:T(2,128)(2,1)}), bf16[32,2,256]{2,1,0:T(2,128)(2,1)S(1)}, u32[]{:S(2)}, u32[]{:S(2)}) async-start(bf16[32,2,256]{2,1,0:T(2,128)(2,1)} %reshape.259), calls=%async_computation | async-start | bytes 65536 | tf_op jit(solution)/shard_map/all_to_all | solution.py:155
  163.3 106.3 %all-gather.6.cloned.1.call-start = ((), (), s32[]{:S(2)}) async-start(), calls=%async_computation.4 | async-start | bytes 4325376 | tf_op jit(solution)/shard_map/all_gather | solution.py:172
  195.7 81.2 %copy-start.9 = (bf16[1,2048,256]{2,1,0:T(8,128)(2,1)S(1)}, bf16[1,2048,256]{2,1,0:T(8,128)(2,1)}, u32[]{:S(2)}) copy-start(bf16[1,2048,256]{2,1,0:T(8,128)(2,1)} %param.29) | copy-start | bytes 3145732
  195.7 316.3 %reduce-scatter.2.cloned.1.call-start = ((), (), s32[]{:S(2)}) async-start(), calls=%async_computation.5 | async-start | bytes 4325376 | tf_op jit(solution)/shard_map/reduce_scatter | solution.py:48
  290.4 236.0 %copy-start.10 = (f32[2048,16]{0,1:T(8,128)S(1)}, f32[2048,16]{0,1:T(8,128)}, u32[]{:S(2)}) copy-start(f32[2048,16]{0,1:T(8,128)} %param.27) | copy-start | bytes 393220
  513.6 22.0 %all-to-all-start.2 = ((bf16[16,2,2048]{2,1,0:T(2,128)(2,1)}), bf16[16,2,2048]{2,1,0:T(2,128)(2,1)S(1)}, u32[]{:S(2)}, u32[]{:S(2)}) async-start(bf16[16,2,2048]{2,1,0:T(2,128)(2,1)} %reshape.243), calls=%async_computation.3 | async-start | bytes 262144 | tf_op jit(solution)/shard_map/all_to_all | solution.py:177
Sparse Core Ops, SparseCore 0:
  73.9 81.2 all-gather.7
  195.8 73.7 all-gather.5
  290.6 221.3 reduce-scatter.1
